TPU v7x, 512 devices: a whole 4x4x16 slice. The times are simulated.
512 devices in a mesh: par: 32 (over z, core), perp: 16 (over x, y).
Axes of the slice: x: 4, y: 4, z: 16, core: 2. Of those that a mesh axis runs over, the one named last changes fastest.
Arguments:
- fields: float32 [2, 32, 8192, 256], P(None, 'par', 'perp'), may hold values from -6 to 6
- weight_bank: float32 [8, 128, 128], replicated, may hold values from -1 to 2, as said below
- dest_slab: int32 [2, 32, 128, 1], P(None, 'par', 'perp'), may hold values from 0 to 15; in each aligned block of 8 rows (0 to 7, 8 to 15, ..., all dimensions but the last counted through in order) at most 2 rows name the same one
- dest_tile: int32 [2, 32, 128], P(None, 'par', 'perp'), may hold values from 0 to 7
- tile_blocks: int32 [2, 32, 128, 2], P(None, 'par', 'perp'), may hold values from 0 to 7
- band_terms: float32 [2, 32], replicated, may hold values from 0.45 to 0.49
Outputs:
- gradient: float32 [2, 32, 8192, 256], P(None, 'par', 'perp')
Inputs may be any that keep to these rules, and one draw needn't show every extreme that they name: `dest_slab`: in each direction and plane, at most 2 of the 8 tiles of one slab name the same destination slab, and in some slab exactly 2 do. `weight_bank`: each block is a dense real matrix.
All inputs are finite; a program needn't handle non-finite values.
Results may differ from a plain program's by a relative error of at most 0.0003.
Values sent between devices are 32-bit elements; how exact they have to be, the bound alone decides.
No kernel may reach another device: no remote copies, remote signals or barrier semaphores. Data moves between devices by JAX's collectives and lax.ppermute only.
A program may use at most 64 MiB of HBM per device.

v0:
```python
import jax
import jax.numpy as jnp
from jax import lax
from jax.sharding import PartitionSpec as P

TILE = 128
PRECISE = lax.Precision.HIGHEST
KAPPA = 0.125


def extended(block, sides, width):
    for axis, dim in sides:
        count = lax.axis_size(axis)
        forward = [(i, i + 1) for i in range(count - 1)]
        backward = [(target, source) for source, target in forward]
        low = lax.ppermute(
            lax.slice_in_dim(block, block.shape[dim] - width, None, axis=dim), axis, forward
        )
        high = lax.ppermute(lax.slice_in_dim(block, 0, width, axis=dim), axis, backward)
        block = jnp.concatenate([low, block, high], axis=dim)
    return block


def split_tiles(plane_pair):
    field_count, row_count, col_count = plane_pair.shape
    shaped = plane_pair.reshape(field_count, row_count // TILE, TILE, col_count // TILE, TILE)
    return shaped.transpose(0, 1, 3, 2, 4).reshape(field_count, -1, TILE, TILE)


def join_tiles(tile_set, row_count, col_count):
    field_count = tile_set.shape[0]
    shaped = tile_set.reshape(field_count, row_count // TILE, col_count // TILE, TILE, TILE)
    return shaped.transpose(0, 1, 3, 2, 4).reshape(field_count, row_count, col_count)


def coefficients(band_terms):
    plane_total = band_terms.shape[1]
    lower, pivots, ratios = ([], [], [])
    previous = jnp.zeros((), jnp.float32)
    for p in range(plane_total):
        lower_now = band_terms[0, p] if p > 0 else jnp.zeros((), jnp.float32)
        upper_now = band_terms[1, p] if p < plane_total - 1 else jnp.zeros((), jnp.float32)
        pivot_now = 1.0 - lower_now * previous
        ratio_now = upper_now / pivot_now
        lower.append(lower_now)
        pivots.append(pivot_now)
        ratios.append(ratio_now)
        previous = ratio_now
    return (lower, pivots, ratios)


def slot_labels(dest_slabs, target, peer_count, capacity):
    tile_count = dest_slabs.shape[-1]
    position = jnp.arange(tile_count, dtype=jnp.int32)
    earlier = position[:, None] > position[None, :]
    shared = dest_slabs[..., :, None] == dest_slabs[..., None, :]
    slot_rank = jnp.sum((shared & earlier).astype(jnp.int32), axis=-1)
    peer_ids = jnp.arange(peer_count, dtype=jnp.int32)
    slot_ids = jnp.arange(capacity, dtype=jnp.int32)
    chosen = (dest_slabs[..., None, None, :] == peer_ids[:, None, None]) & (
        slot_rank[..., None, None, :] == slot_ids[None, :, None]
    )
    return chosen


def local(fields, weight_bank, dest_slab, dest_tile, tile_blocks, band_terms):
    peer_count = lax.axis_size("perp")
    plane_count = lax.axis_size("par")
    row_count = fields.shape[2]
    col_count = fields.shape[3]
    local_pair = fields[:, 0]
    tile_set = split_tiles(local_pair)
    tile_count = tile_set.shape[1]
    capacity = max(2, (tile_count + peer_count - 1) // peer_count)
    dest_slabs = dest_slab[:, 0, :, 0]
    target = dest_tile[:, 0, :]
    left_index = tile_blocks[:, 0, :, 0]
    right_index = tile_blocks[:, 0, :, 1]
    left_block = jnp.take(weight_bank, left_index, axis=0, mode="clip")
    right_block = jnp.take(weight_bank, right_index, axis=0, mode="clip")
    shifted = jnp.einsum("dsij,dsjk->dsik", left_block, tile_set, precision=PRECISE)
    moved = jnp.einsum("dsik,dslk->dsil", shifted, right_block, precision=PRECISE)
    chosen = slot_labels(dest_slabs, target, peer_count, capacity)
    picker = chosen.astype(jnp.float32)
    packed = jnp.einsum("dpcs,dsij->dpcij", picker, moved, precision=PRECISE)
    moved_tiles = lax.all_to_all(packed, "perp", split_axis=1, concat_axis=1, tiled=True)
    all_slabs = lax.all_gather(dest_slabs, "perp", axis=1, tiled=True)
    all_targets = lax.all_gather(target, "perp", axis=1, tiled=True)
    field_count = all_slabs.shape[0]
    all_slabs = all_slabs.reshape(field_count, peer_count, tile_count)
    all_targets = all_targets.reshape(field_count, peer_count, tile_count)
    source_chosen = slot_labels(all_slabs, all_targets, peer_count, capacity)
    me = lax.axis_index("perp")
    mine = source_chosen[:, :, me]
    arrived_target = jnp.sum(mine.astype(jnp.int32) * (all_targets[:, :, None, :] + 1), axis=-1) - 1
    position = jnp.arange(tile_count, dtype=jnp.int32)
    flattened = moved_tiles.reshape(field_count, peer_count * capacity, TILE, TILE)
    flat_target = arrived_target.reshape(field_count, peer_count * capacity)
    landing = (flat_target[:, None, :] == position[None, :, None]).astype(jnp.float32)
    summed = jnp.einsum("dts,dsij->dtij", landing, flattened, precision=PRECISE)
    deposit = join_tiles(summed, row_count, col_count)
    upward = [(i, i + 1) for i in range(plane_count - 1)]
    downward = [(i + 1, i) for i in range(plane_count - 1)]
    mapped = jnp.stack(
        (lax.ppermute(deposit[0], "par", upward), lax.ppermute(deposit[1], "par", downward))
    )
    rimmed = extended(mapped, (("perp", 1),), 1)
    padded = jnp.pad(rimmed, ((0, 0), (0, 0), (1, 1)))
    beside_all = (
        padded[:, 2:, 1:-1] + padded[:, :-2, 1:-1] + padded[:, 1:-1, 2:] + padded[:, 1:-1, :-2]
    )
    smoothed = mapped + KAPPA * (beside_all - 4.0 * mapped)
    orient = jnp.array([1.0, -1.0], jnp.float32)[:, None, None]
    right_side = orient * (local_pair - smoothed)
    lower, pivots, ratios = coefficients(band_terms)
    column_block = lax.all_to_all(
        right_side[:, None], "par", split_axis=2, concat_axis=1, tiled=True
    )
    depth_count = column_block.shape[1]
    eliminated = []
    previous = None
    for p in range(depth_count):
        current = column_block[:, p]
        if previous is not None:
            current = current - lower[p] * previous
        current = current / pivots[p]
        eliminated.append(current)
        previous = current
    solved = [None] * depth_count
    following = None
    for p in reversed(range(depth_count)):
        current = eliminated[p]
        if following is not None:
            current = current - ratios[p] * following
        solved[p] = current
        following = current
    solved = jnp.stack(solved, axis=1)
    result = lax.all_to_all(solved, "par", split_axis=1, concat_axis=2, tiled=True)
    return result


def solution(mesh):
    placed = (
        P(None, "par", "perp", None),
        P(),
        P(None, "par", "perp", None),
        P(None, "par", "perp"),
        P(None, "par", "perp", None),
        P(),
    )
    return jax.shard_map(
        local, mesh=mesh, in_specs=placed, out_specs=P(None, "par", "perp", None), check_vma=False
    )
```

profile of v0, /device:TPU:4, one launch (start us, length us, event | category | flops | bytes accessed | tf_op | source)
XLA Modules:
  0.0 324.2 jit_solution(12230348033059756992)
XLA Ops:
  0.0 0.0 copy-start
  0.0 0.8 slice_reduce_fusion
  0.8 0.1 reshape.112
  0.9 0.1 reshape.104
  1.0 1.7 reshape_squeeze.3
  2.7 0.1 copy.171
  2.8 0.0 copy-done
  2.8 0.0 copy-start.4
  2.8 0.6 gather_fusion
  3.5 1.6 gather_fusion.1
  5.1 0.0 copy-done.4
  5.1 0.1 iota_compare_fusion.2
  5.1 0.2 convert_reduce_fusion.1
  5.4 1.2 fusion.71
  6.5 2.3 convolution_bitcast_fusion
  8.8 2.1 fusion.7
  10.9 3.2 %copy.173 = f32[2,16,2,128,128]{4,3,2,0,1:T(8,128)} copy(f32[2,16,2,128,128]{4,1,3,2,0:T(8,128)S(1)} %fusion.7) | data formatting | bytes 8388608 | tf_op jit(solution)/shard_map/dpcs,dsij->dpcij/dot_general | solution.py:85
  14.2 10.3 %all-to-all-start = ((f32[2,16,2,128,128]{4,3,2,0,1:T(8,128)}), f32[2,16,2,128,128]{4,3,2,0,1:T(8,128)}, u32[]{:S(2)}, u32[]{:S(2)}) async-start(f32[2,16,2,128,128]{4,3,2,0,1:T(8,128)} %copy.173), calls=%async_computation | async-start | bytes 8388608 | tf_op jit(solution)/shard_map/all_to_all | solution.py:86
  24.5 0.1 copy.162
  24.5 0.1 copy.167
  24.6 62.2 %all-gather.1 = s32[2,1,128]{0,1,2:T(1,128)S(1)} all-gather(s32[2,1,8]{0,1,2:T(1,128)S(1)} %copy.167), channel_id=3, replica_groups=mesh['par'=32,'perp'=16] {'perp'}, dimensions={2}, use_global_device_ids=true | all-gather | bytes 1088 | tf_op jit(solution)/shard_map/all_gather | solution.py:88
  86.9 0.1 copy.168
  86.9 0.1 add.40
  87.0 0.1 copy.169
  87.1 23.7 %all-gather = s32[2,1,128,1]{0,3,1,2:T(1,128)S(1)} all-gather(s32[2,1,8,1]{0,3,1,2:T(1,128)S(1)} %copy.162), channel_id=2, replica_groups=mesh['par'=32,'perp'=16] {'perp'}, dimensions={2}, use_global_device_ids=true | all-gather | bytes 1088 | tf_op jit(solution)/shard_map/all_gather | solution.py:87
  110.8 0.1 copy.164
  111.0 0.1 convert_reduce_fusion
  111.1 0.1 copy.170
  111.2 0.1 sub.1780
  111.3 0.0 all-to-all-done
  111.3 2.5 copy.174
  113.8 3.9 %fusion = f32[2,8,128,128]{3,1,2,0:T(8,128)S(1)} fusion(f32[2,32,128,128]{3,2,1,0:T(8,128)S(1)} %bitcast.114, s32[2,32]{1,0:T(2,128)S(1)} %sub.1780), kind=kOutput, calls=%fused_computation.2 | convolution fusion | flops 100663808 | bytes 5243136 | tf_op jit(solution)/shard_map/dts,dsij->dtij/dot_general | solution.py:100
  117.6 0.4 fusion.66
  118.0 0.2 copy.176
  118.2 1.3 collective-permute-start
  119.6 0.2 copy.177
  119.8 1.3 collective-permute-start.1
  121.1 0.0 collective-permute-done
  121.1 0.4 stack.8
  121.5 17.7 %collective-permute-done.1 = f32[512,256]{1,0:T(8,128)S(1)} collective-permute-done((f32[512,256]{1,0:T(8,128)S(1)}, f32[512,256]{1,0:T(8,128)S(1)}, u32[]{:S(2)}, u32[]{:S(2)}) %collective-permute-start.1) | collective-permute-done | bytes 524320 | tf_op jit(solution)/shard_map/ppermute | solution.py:105
  139.1 0.4 stack.9
  139.5 0.0 copy-start.2
  139.5 0.0 copy-start.6
  139.5 4.1 %collective-permute-start.2 = (f32[2,1,256]{2,0,1:T(2,128)S(1)}, f32[2,1,256]{2,0,1:T(2,128)S(1)}, u32[]{:S(2)}, u32[]{:S(2)}) collective-permute-start(f32[2,1,256]{2,0,1:T(2,128)S(1)} %get-tuple-element.71), channel_id=1, source_target_pairs={{1,0},{2,1},{3,2},{4,3},{5,4},{6,5},{7,6},{8,7},{9,8},{10,9},{11,1... | collective-permute-start | bytes 6152 | tf_op jit(solution)/shard_map/ppermute | solution.py:19
  143.7 1.9 collective-permute-start.3
  145.6 0.0 collective-permute-done.2
  145.6 5.6 %collective-permute-done.3 = f32[2,1,256]{2,0,1:T(2,128)S(1)} collective-permute-done((f32[2,1,256]{2,0,1:T(2,128)S(1)}, f32[2,1,256]{2,0,1:T(2,128)S(1)}, u32[]{:S(2)}, u32[]{:S(2)}) %collective-permute-start.3) | collective-permute-done | bytes 2080 | tf_op jit(solution)/shard_map/ppermute | solution.py:16
  151.2 5.3 %select_maximum_fusion = f32[2,514,258]{2,0,1:T(2,128)S(1)} fusion(f32[2,1,256]{2,0,1:T(2,128)S(1)} %collective-permute-done.2, f32[2,1,256]{2,0,1:T(2,128)S(1)} %collective-permute-done.3, f32[1,512,256]{2,0,1:T(1,128)S(1)} %stack.9, f32[1,512,256]{2,0,1:T(1,128)S(1)} %stack.8), kind=kLoop, calls=%fused_computation.5 | loop fusion | flops 2652240 | bytes 2113568 | tf_op jit(solution)/shard_map/concatenate | solution.py:20
  156.5 0.0 copy-done.2
  156.5 0.0 copy-done.6
  156.5 6.2 %multiply_bitcast_fusion = f32[2,1,512,256]{3,0,1,2:T(2,128)} fusion(f32[2,514,258]{2,0,1:T(2,128)S(1)} %select_maximum_fusion, f32[1,512,256]{2,0,1:T(1,128)S(1)} %stack.9, f32[1,512,256]{2,0,1:T(1,128)S(1)} %stack.8, f32[2,1,256]{2,0,1:T(2,128)S(1)} %collective-permute-done.3, f32[2,1,256]{2,0,1:T(2,128)S(1)} %collective-permute-done.2, ...), kind=kLoop, calls=%fused_computation.27 | loop fusion | flops 3670016 | bytes 5246984 | tf_op jit(solution)/shard_map/broadcast_in_dim | solution.py:117
  162.7 22.1 %all-to-all-start.1 = ((f32[2,1,512,256]{3,0,1,2:T(2,128)}), f32[2,1,512,256]{3,0,1,2:T(2,128)S(1)}, u32[]{:S(2)}, u32[]{:S(2)}) async-start(f32[2,1,512,256]{3,0,1,2:T(2,128)} %multiply_bitcast_fusion), calls=%async_computation.1 | async-start | bytes 2097152 | tf_op jit(solution)/shard_map/all_to_all | solution.py:116
  184.9 0.7 fusion.70
  188.6 0.7 fusion.69
  200.8 0.7 fusion.68
  212.9 0.7 fusion.67
  226.6 14.0 %all-to-all-done.1 = f32[2,1,512,256]{3,0,1,2:T(2,128)S(1)} async-done(((f32[2,1,512,256]{3,0,1,2:T(2,128)}), f32[2,1,512,256]{3,0,1,2:T(2,128)S(1)}, u32[]{:S(2)}, u32[]{:S(2)}) %all-to-all-start.1) | async-done | bytes 1048608 | tf_op jit(solution)/shard_map/all_to_all | solution.py:116
  240.6 0.2 fusion.65
  240.8 0.2 fusion.64
  241.1 20.9 %constant_dynamic-update-slice_fusion.31 = (f32[2,32,16,256]{3,2,0,1:T(8,128)S(1)}, f32[2,1,16,256]{3,2,0,1:T(8,128)S(1)}, f32[2,1,16,256]{3,2,0,1:T(8,128)S(1)}...) fusion(f32[2,1,16,256]{3,0,2,1:T(2,128)S(1)} %get-tuple-element, ...), kind=kLoop, calls=%fused_computation.62 | loop fusion | flops 1269759 | bytes 2064756
  262.4 0.6 constant_dynamic-update-slice_fusion.1
  263.1 0.6 constant_dynamic-update-slice_fusion
  263.7 59.5 %all_to_all.29 = f32[2,32,16,256]{3,2,0,1:T(8,128)S(1)} all-to-all(f32[2,32,16,256]{3,2,0,1:T(8,128)S(1)} %constant_dynamic-update-slice_fusion), channel_id=1, replica_groups=mesh['par'=32,'perp'=16] {'par'}, dimensions={1} | all-to-all | bytes 2097152 | tf_op jit(solution)/shard_map/all_to_all | solution.py:138
  323.2 1.1 copy.210
  (47 shorter events, 0.4 us)
Async XLA Ops:
  0.0 2.8 copy-start
  2.8 2.2 copy-start.4
  5.1 1.4 copy-start.1
  14.2 10.4 %copy-start.5 = (s32[2,1,8]{2,1,0:T(1,128)S(1)}, s32[2,1,8]{2,1,0:T(1,128)}, u32[]{:S(2)}) copy-start(s32[2,1,8]{2,1,0:T(1,128)} %param.10) | copy-start | bytes 196
  14.2 97.1 %all-to-all-start = ((f32[2,16,2,128,128]{4,3,2,0,1:T(8,128)}), f32[2,16,2,128,128]{4,3,2,0,1:T(8,128)}, u32[]{:S(2)}, u32[]{:S(2)}) async-start(f32[2,16,2,128,128]{4,3,2,0,1:T(8,128)} %copy.173), calls=%async_computation | async-start | bytes 8388608 | tf_op jit(solution)/shard_map/all_to_all | solution.py:86
  118.2 2.9 collective-permute-start
  119.8 19.3 %collective-permute-start.1 = (f32[512,256]{1,0:T(8,128)S(1)}, f32[512,256]{1,0:T(8,128)S(1)}, u32[]{:S(2)}, u32[]{:S(2)}) collective-permute-start(f32[512,256]{1,0:T(8,128)S(1)} %bitcast.125), channel_id=1, source_target_pairs={{16,0},{32,16},{48,32},{64,48},{80,64},{96,80},{112,96},{128,112},... | collective-permute-start | bytes 1572872 | tf_op jit(solution)/shard_map/ppermute | solution.py:105
  139.5 17.0 %copy-start.2 = (f32[2,1,512,256]{3,2,1,0:T(8,128)S(1)}, f32[2,1,512,256]{3,2,1,0:T(8,128)}, u32[]{:S(2)}) copy-start(f32[2,1,512,256]{3,2,1,0:T(8,128)} %param.7) | copy-start | bytes 3145732
  139.5 17.0 %copy-start.6 = (f32[2]{0:T(128)S(1)}, f32[2]{0:T(128)}, u32[]{:S(2)}) copy-start(f32[2]{0:T(128)} %constant.25.clone) | copy-start | bytes 28
  139.5 6.0 %collective-permute-start.2 = (f32[2,1,256]{2,0,1:T(2,128)S(1)}, f32[2,1,256]{2,0,1:T(2,128)S(1)}, u32[]{:S(2)}, u32[]{:S(2)}) collective-permute-start(f32[2,1,256]{2,0,1:T(2,128)S(1)} %get-tuple-element.71), channel_id=1, source_target_pairs={{1,0},{2,1},{3,2},{4,3},{5,4},{6,5},{7,6},{8,7},{9,8},{10,9},{11,1... | collective-permute-start | bytes 6152 | tf_op jit(solution)/shard_map/ppermute | solution.py:19
  143.7 7.6 %collective-permute-start.3 = (f32[2,1,256]{2,0,1:T(2,128)S(1)}, f32[2,1,256]{2,0,1:T(2,128)S(1)}, u32[]{:S(2)}, u32[]{:S(2)}) collective-permute-start(f32[2,1,256]{2,0,1:T(2,128)S(1)} %get-tuple-element.70), channel_id=1, source_target_pairs={{0,1},{1,2},{2,3},{3,4},{4,5},{5,6},{6,7},{7,8},{8,9},{9,10},{10,1... | collective-permute-start | bytes 6152 | tf_op jit(solution)/shard_map/ppermute | solution.py:16
  162.7 22.1 %copy-start.3 = (f32[2,32]{1,0:T(2,128)S(1)}, f32[2,32]{1,0:T(2,128)}, u32[]{:S(2)}) copy-start(f32[2,32]{1,0:T(2,128)} %param.12) | copy-start | bytes 772
  162.7 77.9 %all-to-all-start.1 = ((f32[2,1,512,256]{3,0,1,2:T(2,128)}), f32[2,1,512,256]{3,0,1,2:T(2,128)S(1)}, u32[]{:S(2)}, u32[]{:S(2)}) async-start(f32[2,1,512,256]{3,0,1,2:T(2,128)} %multiply_bitcast_fusion), calls=%async_computation.1 | async-start | bytes 2097152 | tf_op jit(solution)/shard_map/all_to_all | solution.py:116
where the time goes:
time: 326 us; the launch traced here: 324 us
  blocking collectives  145 us (44%)
  starting transfers between devices  41.1 us (13%)
  between operations  39.5 us (12%)
  waiting for transfers between devices  37.3 us (11%)
  other arithmetic  34.2 us (10%)
  local copies, waits for them, and re-layouts  17.3 us (5%)
  matrix products  9.36 us (3%)
    all_gather x1, blocking collectives, local(): all_targets = lax.all_gather(target, 'perp', axis=1, tiled=True)  62.2 us
    all_to_all x1, blocking collectives, local(): lax.all_to_all(solved, 'par', split_axis=1, concat_axis=2, tiled=True)  59.5 us
    all_gather x1, blocking collectives, local(): all_slabs = lax.all_gather(dest_slabs, 'perp', axis=1, tiled=True)  23.7 us
    all_to_all x1, starting transfers between devices, local(): lax.all_to_all(right_side[:, None], 'par', split_axis=2, concat_axis=1, t...  22.1 us
    unnamed x16, other arithmetic  21.7 us
    ppermute x1, waiting for transfers between devices, local(): lax.ppermute(deposit[1], 'par', downward)  17.7 us
    all_to_all x1, waiting for transfers between devices, local(): lax.all_to_all(right_side[:, None], 'par', split_axis=2, concat_axis=1, t...  14 us
    all_to_all x1, starting transfers between devices, local(): lax.all_to_all(packed, 'perp', split_axis=1, concat_axis=1, tiled=True)  10.3 us
  transfers between devices with their start and end apart: 6, of which 3 were waited for; matrix products, arithmetic and copies ran while one was open for 1% of the time, Pallas kernels for 0%

commit v1 on v0

--- a/solution.py
+++ b/solution.py
@@ -85,7 +85,9 @@
     packed = jnp.einsum("dpcs,dsij->dpcij", picker, moved, precision=PRECISE)
     moved_tiles = lax.all_to_all(packed, "perp", split_axis=1, concat_axis=1, tiled=True)
     all_slabs = lax.all_gather(dest_slabs, "perp", axis=1, tiled=True)
-    all_targets = lax.all_gather(target, "perp", axis=1, tiled=True)
+    all_targets = jnp.concatenate(
+        lax.all_to_all(jnp.stack([target] * lax.axis_size("perp")), "perp", 0, 0), axis=1
+    )
     field_count = all_slabs.shape[0]
     all_slabs = all_slabs.reshape(field_count, peer_count, tile_count)
     all_targets = all_targets.reshape(field_count, peer_count, tile_count)

time: 326 us -> 304 us (0.933)
  the two profiles are of different devices: /device:TPU:4 before, /device:TPU:2 now
where the time goes in v1:
time: 304 us; the launch traced here: 302 us
  blocking collectives  123 us (40%)
  starting transfers between devices  47.2 us (16%)
  between operations  39.5 us (13%)
  other arithmetic  34.3 us (11%)
  waiting for transfers between devices  30.6 us (10%)
  local copies, waits for them, and re-layouts  18.4 us (6%)
  matrix products  9.38 us (3%)
    all_gather x1, blocking collectives, local(): all_slabs = lax.all_gather(dest_slabs, 'perp', axis=1, tiled=True)  63.6 us
    all_to_all x1, blocking collectives, local(): lax.all_to_all(solved, 'par', split_axis=1, concat_axis=2, tiled=True)  59.5 us
    all_to_all x1, starting transfers between devices, local(): lax.all_to_all(right_side[:, None], 'par', split_axis=2, concat_axis=1, t...  22.1 us
    unnamed x16, other arithmetic  21.7 us
    all_to_all x1, waiting for transfers between devices, local(): lax.all_to_all(right_side[:, None], 'par', split_axis=2, concat_axis=1, t...  14 us
    ppermute x1, waiting for transfers between devices, local(): lax.ppermute(deposit[1], 'par', downward)  11.8 us
    all_to_all x1, starting transfers between devices, local(): lax.all_to_all(jnp.stack([target] * lax.axis_size('perp')), 'perp', 0, 0)  9.18 us
    all_to_all x1, starting transfers between devices, local(): lax.all_to_all(packed, 'perp', split_axis=1, concat_axis=1, tiled=True)  7.26 us
  transfers between devices with their start and end apart: 7, of which 3 were waited for; matrix products, arithmetic and copies ran while one was open for 6% of the time, Pallas kernels for 0%

profile of v1, /device:TPU:2, one launch (start us, length us, event | category | flops | bytes accessed | tf_op | source)
XLA Modules:
  0.0 302.4 jit_solution(6735869032401068307)
XLA Ops:
  0.0 0.0 copy-start
  0.0 1.3 stack.10
  1.3 9.2 %all-to-all-start = ((s32[16,2,8]{2,1,0:T(2,128)}), s32[16,2,8]{2,1,0:T(2,128)S(1)}, u32[]{:S(2)}, u32[]{:S(2)}) async-start(s32[16,2,8]{2,1,0:T(2,128)} %stack.10), calls=%async_computation | async-start | bytes 32768 | tf_op jit(solution)/shard_map/all_to_all | solution.py:89
  10.5 0.8 slice_reduce_fusion
  11.3 0.1 reshape.108
  11.4 0.1 reshape.100
  11.5 1.7 reshape_squeeze.3
  13.2 0.1 copy.116
  13.3 0.0 copy-done
  13.4 0.0 copy-start.4
  13.4 0.6 gather_fusion
  14.0 1.6 gather_fusion.1
  15.6 0.0 copy-done.4
  15.6 0.1 iota_compare_fusion.2
  15.7 0.2 convert_reduce_fusion.1
  15.9 1.2 fusion.71
  17.0 0.0 copy-done.1
  17.0 2.3 convolution_bitcast_fusion
  19.3 2.1 fusion.7
  21.4 3.2 %copy.118 = f32[2,16,2,128,128]{4,3,2,0,1:T(8,128)} copy(f32[2,16,2,128,128]{4,1,3,2,0:T(8,128)S(1)} %fusion.7) | data formatting | bytes 8388608 | tf_op jit(solution)/shard_map/dpcs,dsij->dpcij/dot_general | solution.py:85
  24.7 0.0 all-to-all-done
  24.7 7.3 %all-to-all-start.1 = ((f32[2,16,2,128,128]{4,3,2,0,1:T(8,128)}), f32[2,16,2,128,128]{4,3,2,0,1:T(8,128)}, u32[]{:S(2)}, u32[]{:S(2)}) async-start(f32[2,16,2,128,128]{4,3,2,0,1:T(8,128)} %copy.118), calls=%async_computation.1 | async-start | bytes 8388608 | tf_op jit(solution)/shard_map/all_to_all | solution.py:86
  31.9 0.1 copy.109
  32.0 63.6 %all-gather = s32[2,1,128,1]{0,3,1,2:T(1,128)S(1)} all-gather(s32[2,1,8,1]{0,3,1,2:T(1,128)S(1)} %copy.109), channel_id=2, replica_groups=mesh['par'=32,'perp'=16] {'perp'}, dimensions={2}, use_global_device_ids=true | all-gather | bytes 1088 | tf_op jit(solution)/shard_map/all_gather | solution.py:87
  95.6 0.1 copy.111
  95.8 0.1 convert_reduce_fusion
  95.9 0.1 copy.114
  96.0 0.1 copy.115
  96.1 0.1 sub.1780
  96.2 0.0 all-to-all-done.1
  96.2 2.5 copy.119
  98.7 3.9 %fusion = f32[2,8,128,128]{3,1,2,0:T(8,128)S(1)} fusion(f32[2,32,128,128]{3,2,1,0:T(8,128)S(1)} %bitcast.115, s32[2,32]{1,0:T(2,128)S(1)} %sub.1780), kind=kOutput, calls=%fused_computation.2 | convolution fusion | flops 100663808 | bytes 5243136 | tf_op jit(solution)/shard_map/dts,dsij->dtij/dot_general | solution.py:102
  102.5 0.4 fusion.66
  102.9 0.2 copy.121
  103.1 1.3 collective-permute-start
  104.4 0.2 copy.122
  104.7 1.3 collective-permute-start.1
  106.0 0.0 collective-permute-done
  106.0 0.4 stack.11
  106.3 11.8 %collective-permute-done.1 = f32[512,256]{1,0:T(8,128)S(1)} collective-permute-done((f32[512,256]{1,0:T(8,128)S(1)}, f32[512,256]{1,0:T(8,128)S(1)}, u32[]{:S(2)}, u32[]{:S(2)}) %collective-permute-start.1) | collective-permute-done | bytes 524320 | tf_op jit(solution)/shard_map/ppermute | solution.py:107
  118.1 0.4 stack.12
  118.5 0.0 copy-start.2
  118.5 0.0 copy-start.5
  118.5 3.2 %collective-permute-start.2 = (f32[2,1,256]{2,0,1:T(2,128)S(1)}, f32[2,1,256]{2,0,1:T(2,128)S(1)}, u32[]{:S(2)}, u32[]{:S(2)}) collective-permute-start(f32[2,1,256]{2,0,1:T(2,128)S(1)} %get-tuple-element.71), channel_id=1, source_target_pairs={{1,0},{2,1},{3,2},{4,3},{5,4},{6,5},{7,6},{8,7},{9,8},{10,9},{11,1... | collective-permute-start | bytes 6152 | tf_op jit(solution)/shard_map/ppermute | solution.py:19
  121.7 2.8 collective-permute-start.3
  124.5 0.0 collective-permute-done.2
  124.5 4.8 %collective-permute-done.3 = f32[2,1,256]{2,0,1:T(2,128)S(1)} collective-permute-done((f32[2,1,256]{2,0,1:T(2,128)S(1)}, f32[2,1,256]{2,0,1:T(2,128)S(1)}, u32[]{:S(2)}, u32[]{:S(2)}) %collective-permute-start.3) | collective-permute-done | bytes 2080 | tf_op jit(solution)/shard_map/ppermute | solution.py:16
  129.3 5.3 %select_maximum_fusion = f32[2,514,258]{2,0,1:T(2,128)S(1)} fusion(f32[2,1,256]{2,0,1:T(2,128)S(1)} %collective-permute-done.2, f32[2,1,256]{2,0,1:T(2,128)S(1)} %collective-permute-done.3, f32[1,512,256]{2,0,1:T(1,128)S(1)} %stack.12, f32[1,512,256]{2,0,1:T(1,128)S(1)} %stack.11), kind=kLoop, calls=%fused_computation.5 | loop fusion | flops 2652240 | bytes 2113568 | tf_op jit(solution)/shard_map/concatenate | solution.py:20
  134.6 0.0 copy-done.2
  134.6 0.0 copy-done.5
  134.6 6.2 %multiply_bitcast_fusion = f32[2,1,512,256]{3,0,1,2:T(2,128)} fusion(f32[2,514,258]{2,0,1:T(2,128)S(1)} %select_maximum_fusion, f32[1,512,256]{2,0,1:T(1,128)S(1)} %stack.12, f32[1,512,256]{2,0,1:T(1,128)S(1)} %stack.11, f32[2,1,256]{2,0,1:T(2,128)S(1)} %collective-permute-done.3, f32[2,1,256]{2,0,1:T(2,128)S(1)} %collective-permute-done.2, ...), kind=kLoop, calls=%fused_computation.27 | loop fusion | flops 3670016 | bytes 5246984 | tf_op jit(solution)/shard_map/broadcast_in_dim | solution.py:119
  140.8 22.1 %all-to-all-start.2 = ((f32[2,1,512,256]{3,0,1,2:T(2,128)}), f32[2,1,512,256]{3,0,1,2:T(2,128)S(1)}, u32[]{:S(2)}, u32[]{:S(2)}) async-start(f32[2,1,512,256]{3,0,1,2:T(2,128)} %multiply_bitcast_fusion), calls=%async_computation.2 | async-start | bytes 2097152 | tf_op jit(solution)/shard_map/all_to_all | solution.py:118
  163.0 0.7 fusion.70
  166.7 0.7 fusion.69
  178.9 0.7 fusion.68
  191.0 0.7 fusion.67
  204.7 14.0 %all-to-all-done.2 = f32[2,1,512,256]{3,0,1,2:T(2,128)S(1)} async-done(((f32[2,1,512,256]{3,0,1,2:T(2,128)}), f32[2,1,512,256]{3,0,1,2:T(2,128)S(1)}, u32[]{:S(2)}, u32[]{:S(2)}) %all-to-all-start.2) | async-done | bytes 1048608 | tf_op jit(solution)/shard_map/all_to_all | solution.py:118
  218.7 0.2 fusion.65
  218.9 0.2 fusion.64
  219.1 20.9 %constant_dynamic-update-slice_fusion.31 = (f32[2,32,16,256]{3,2,0,1:T(8,128)S(1)}, f32[2,1,16,256]{3,2,0,1:T(8,128)S(1)}, f32[2,1,16,256]{3,2,0,1:T(8,128)S(1)}...) fusion(f32[2,1,16,256]{3,0,2,1:T(2,128)S(1)} %get-tuple-element, ...), kind=kLoop, calls=%fused_computation.62 | loop fusion | flops 1269759 | bytes 2064756
  240.5 0.6 constant_dynamic-update-slice_fusion.1
  241.2 0.6 constant_dynamic-update-slice_fusion
  241.8 59.5 %all_to_all.34 = f32[2,32,16,256]{3,2,0,1:T(8,128)S(1)} all-to-all(f32[2,32,16,256]{3,2,0,1:T(8,128)S(1)} %constant_dynamic-update-slice_fusion), channel_id=1, replica_groups=mesh['par'=32,'perp'=16] {'par'}, dimensions={1} | all-to-all | bytes 2097152 | tf_op jit(solution)/shard_map/all_to_all | solution.py:140
  301.3 1.1 copy.155
  (44 shorter events, 0.4 us)
Async XLA Ops:
  0.0 13.3 %copy-start = (f32[8,128,128]{2,1,0:T(8,128)S(1)}, f32[8,128,128]{2,1,0:T(8,128)}, u32[]{:S(2)}) copy-start(f32[8,128,128]{2,1,0:T(8,128)} %param.8) | copy-start | bytes 1572868
  1.3 23.3 %all-to-all-start = ((s32[16,2,8]{2,1,0:T(2,128)}), s32[16,2,8]{2,1,0:T(2,128)S(1)}, u32[]{:S(2)}, u32[]{:S(2)}) async-start(s32[16,2,8]{2,1,0:T(2,128)} %stack.10), calls=%async_computation | async-start | bytes 32768 | tf_op jit(solution)/shard_map/all_to_all | solution.py:89
  13.4 2.2 copy-start.4
  15.7 1.4 copy-start.1
  24.7 71.5 %all-to-all-start.1 = ((f32[2,16,2,128,128]{4,3,2,0,1:T(8,128)}), f32[2,16,2,128,128]{4,3,2,0,1:T(8,128)}, u32[]{:S(2)}, u32[]{:S(2)}) async-start(f32[2,16,2,128,128]{4,3,2,0,1:T(8,128)} %copy.118), calls=%async_computation.1 | async-start | bytes 8388608 | tf_op jit(solution)/shard_map/all_to_all | solution.py:86
  103.1 2.9 collective-permute-start
  104.7 13.4 %collective-permute-start.1 = (f32[512,256]{1,0:T(8,128)S(1)}, f32[512,256]{1,0:T(8,128)S(1)}, u32[]{:S(2)}, u32[]{:S(2)}) collective-permute-start(f32[512,256]{1,0:T(8,128)S(1)} %bitcast.126), channel_id=1, source_target_pairs={{16,0},{32,16},{48,32},{64,48},{80,64},{96,80},{112,96},{128,112},... | collective-permute-start | bytes 1572872 | tf_op jit(solution)/shard_map/ppermute | solution.py:107
  118.5 16.1 %copy-start.2 = (f32[2,1,512,256]{3,2,1,0:T(8,128)S(1)}, f32[2,1,512,256]{3,2,1,0:T(8,128)}, u32[]{:S(2)}) copy-start(f32[2,1,512,256]{3,2,1,0:T(8,128)} %param.7) | copy-start | bytes 3145732
  118.5 16.1 %copy-start.5 = (f32[2]{0:T(128)S(1)}, f32[2]{0:T(128)}, u32[]{:S(2)}) copy-start(f32[2]{0:T(128)} %constant.25.clone) | copy-start | bytes 28
  118.5 6.0 %collective-permute-start.2 = (f32[2,1,256]{2,0,1:T(2,128)S(1)}, f32[2,1,256]{2,0,1:T(2,128)S(1)}, u32[]{:S(2)}, u32[]{:S(2)}) collective-permute-start(f32[2,1,256]{2,0,1:T(2,128)S(1)} %get-tuple-element.71), channel_id=1, source_target_pairs={{1,0},{2,1},{3,2},{4,3},{5,4},{6,5},{7,6},{8,7},{9,8},{10,9},{11,1... | collective-permute-start | bytes 6152 | tf_op jit(solution)/shard_map/ppermute | solution.py:19
  121.7 7.6 %collective-permute-start.3 = (f32[2,1,256]{2,0,1:T(2,128)S(1)}, f32[2,1,256]{2,0,1:T(2,128)S(1)}, u32[]{:S(2)}, u32[]{:S(2)}) collective-permute-start(f32[2,1,256]{2,0,1:T(2,128)S(1)} %get-tuple-element.70), channel_id=1, source_target_pairs={{0,1},{1,2},{2,3},{3,4},{4,5},{5,6},{6,7},{7,8},{8,9},{9,10},{10,1... | collective-permute-start | bytes 6152 | tf_op jit(solution)/shard_map/ppermute | solution.py:16
  140.8 22.2 %copy-start.3 = (f32[2,32]{1,0:T(2,128)S(1)}, f32[2,32]{1,0:T(2,128)}, u32[]{:S(2)}) copy-start(f32[2,32]{1,0:T(2,128)} %param.12) | copy-start | bytes 772
  140.8 77.9 %all-to-all-start.2 = ((f32[2,1,512,256]{3,0,1,2:T(2,128)}), f32[2,1,512,256]{3,0,1,2:T(2,128)S(1)}, u32[]{:S(2)}, u32[]{:S(2)}) async-start(f32[2,1,512,256]{3,0,1,2:T(2,128)} %multiply_bitcast_fusion), calls=%async_computation.2 | async-start | bytes 2097152 | tf_op jit(solution)/shard_map/all_to_all | solution.py:118
